TPU v7x, 128 devices: a whole 4x4x4 slice. The times are simulated.
128 devices in a mesh: date: 16 (over z, x), space: 8 (over y, core).
Axes of the slice: x: 4, y: 4, z: 4, core: 2. Of those that a mesh axis runs over, the one named last changes fastest.
Arguments:
- frames: bfloat16 [64, 2048, 1024], P('date', 'space'), may hold values from -6 to 6
- cloud_mask: int32 [64, 2048], P('date', 'space'), may hold values from 0 to 1
- qkv_weight: bfloat16 [2, 1024, 3072], replicated, may hold values from -0.1875 to 0.1875
- out_weight: bfloat16 [2, 1024, 1024], replicated, may hold values from -0.1875 to 0.1875
- norm_gain: float32 [2, 1024], replicated, may hold values from 0.1 to 1.9
- head_norm_scale: float32 [2, 1024], replicated, may hold values from 0.1 to 1.9
- decay: float32 [2, 64, 16], P(None, 'date'), as said below
Outputs:
- forecast: bfloat16 [64, 2048, 1024], P('date', 'space')
Inputs may be any that keep to these rules, and one draw needn't show every extreme that they name: `decay`: every entry lies strictly between 0 and 1.
All inputs are finite; a program needn't handle non-finite values.
Results may differ from a plain program's by a relative error of at most 0.0065.
Values may be sent and summed in bfloat16 or wider, within the bound.
No kernel may reach another device: no remote copies, remote signals or barrier semaphores. Data moves between devices by JAX's collectives and lax.ppermute only.
A program may use at most 128 MiB of HBM per device.

v0:
```python
import jax
import jax.numpy as jnp
from jax import lax
from jax.sharding import PartitionSpec as P

HEADS = 16
HEAD = 64
STACK_LEVELS = 2


def carried_in(value, axis, join, neutral):
    count, mine = (lax.axis_size(axis), lax.axis_index(axis))
    pieces = jax.tree.map(lambda part: lax.all_gather(part, axis), value)
    subtotal = jax.tree.map(
        lambda part, zero: jnp.full_like(part, 0) + jnp.asarray(zero, part.dtype), value, neutral
    )

    def step(position, subtotal):
        longer = join(subtotal, jax.tree.map(lambda part: part[position], pieces))
        return jax.tree.map(lambda new, old: jnp.where(position < mine, new, old), longer, subtotal)

    return lax.fori_loop(0, count - 1, step, subtotal)


def feature(u):
    return jax.nn.elu(u) + 1.0


def chain(earlier, later):
    return (earlier[0] * later[1][:, None, None] + later[0], earlier[1] * later[1])


def shards(frames, cloud_mask, qkv_weight, out_weight, norm_gain, head_norm_scale, decay):
    dates_here, tokens_here, width = frames.shape
    heads = HEADS
    current = frames
    flag_f = cloud_mask.astype(jnp.float32)[:, :, None]
    for layer in range(STACK_LEVELS):
        xf = current.astype(jnp.float32)
        in_msq = jnp.mean(xf * xf, -1, keepdims=True) + 1e-05
        normalized_output = (xf * lax.rsqrt(in_msq) * norm_gain[layer]).astype(jnp.bfloat16)
        proj = jnp.dot(
            normalized_output.reshape(-1, width),
            qkv_weight[layer],
            preferred_element_type=jnp.float32,
        )
        proj = proj.reshape(dates_here, tokens_here, 3 * width)
        query = (
            feature(proj[:, :, :width])
            .astype(jnp.bfloat16)
            .reshape(dates_here, tokens_here, heads, HEAD)
        )
        key = (
            (feature(proj[:, :, width : 2 * width]) * flag_f)
            .astype(jnp.bfloat16)
            .reshape(dates_here, tokens_here, heads, HEAD)
        )
        value = (
            proj[:, :, 2 * width :]
            .astype(jnp.bfloat16)
            .reshape(dates_here, tokens_here, heads, HEAD)
        )
        pairing_partial = jnp.einsum(
            "tshe,tshf->thef", key, value, preferred_element_type=jnp.float32
        )
        kv = lax.psum(pairing_partial, "space")
        persist_factor = decay[layer]

        def advance(state, inputs):
            state = inputs[1][:, None, None] * state + inputs[0]
            return (state, state)

        start = jnp.zeros((heads, HEAD, HEAD), jnp.float32)
        last_state, local_states = lax.scan(advance, start, (kv, persist_factor))
        kept = jnp.cumprod(persist_factor, axis=0)
        total_kept = kept[-1]
        incoming, _ = carried_in(
            (last_state, total_kept),
            "date",
            chain,
            (jnp.zeros_like(last_state), jnp.ones_like(total_kept)),
        )
        states = local_states + kept[:, :, None, None] * incoming[None]
        state_b = states.astype(jnp.bfloat16)
        numer = jnp.einsum("tshe,thef->tshf", query, state_b, preferred_element_type=jnp.float32)
        head_msq = jnp.mean(numer * numer, -1, keepdims=True) + 1e-05
        numer = numer * lax.rsqrt(head_msq)
        mixed = (numer.reshape(dates_here, tokens_here, width) * head_norm_scale[layer]).astype(
            jnp.bfloat16
        )
        update = jnp.dot(
            mixed.reshape(-1, width), out_weight[layer], preferred_element_type=jnp.float32
        )
        current = (xf + update.reshape(dates_here, tokens_here, width)).astype(jnp.bfloat16)
    return current


def solution(mesh):
    placed = (
        P("date", "space", None),
        P("date", "space"),
        P(),
        P(),
        P(),
        P(),
        P(None, "date", None),
    )
    return jax.shard_map(
        shards, mesh=mesh, in_specs=placed, out_specs=P("date", "space", None), check_vma=False
    )
```

profile of v0, /device:TPU:1, one launch (start us, length us, event | category | flops | bytes accessed | tf_op | source)
XLA Modules:
  0.0 406.9 jit_solution(10266856537543714752)
XLA Ops:
  7.4 2.1 fusion.10
  9.5 8.9 %fusion.6 = f32[4,256,3072]{2,1,0:T(8,128)S(1)} fusion(bf16[2,1024,3072]{2,1,0:T(8,128)(2,1)} %param.17, bf16[4,256,1024]{2,1,0:T(8,128)(2,1)S(1)} %copy-done.4, f32[1024]{0:T(1024)S(1)} %bitcast.125, f32[4,256]{1,0:T(4,128)S(1)} %add_rsqrt_fusion.3), kind=kOutput, calls=%fused_computation.26 | convolution fusion | flops 6446645248 | bytes 20979712 | tf_op jit(solution)/shard_map/dot_general | solution.py:42
  18.4 1.7 slice.113
  20.1 5.1 %fusion.21 = (bf16[4,256,1024]{2,1,0:T(8,128)(2,1)}, bf16[4,256,1024]{2,1,0:T(8,128)(2,1)}) fusion(f32[4,256,3072]{2,1,0:T(8,128)S(1)} %fusion.6, f32[4,256]{1,0:T(4,128)S(1)} %convert_element_type.59), kind=kLoop, calls=%fused_computation.47 | loop fusion | flops 11534336 | bytes 12587008 | tf_op jit(solution)/shard_map/convert_element_type | solution.py:55
  25.2 2.8 copy.28
  28.0 3.9 copy.29
  32.0 3.6 fusion.61
  36.3 66.5 %all-reduce.3.cloned.1.call-done = f32[4,16,64,64]{3,2,1,0:T(8,128)} async-done(((f32[4,16,64,64]{3,2,1,0:T(8,128)}), f32[4,16,64,64]{3,2,1,0:T(8,128)}) %all-reduce.3.cloned.1.call-update) | async-done | bytes 1048592 | tf_op jit(solution)/shard_map/psum | solution.py:66
  103.0 4.9 %while.54 = (s32[]{:T(128)}, f32[16,64,64]{2,1,0:T(8,128)S(1)}, f32[4,16,64,64]{3,2,1,0:T(8,128)S(1)}, f32[4,16]{1,0:T(4,128)S(1)}, f32[4,16,64,64]{3,2,1,0:T(8,128)}, /*index=5*/s32[]{:T(128)}, s32[]{:T(128)}) while((s32[]{:T(128)}, f32[16,64,64]{2,1,0:T(8,128)S(1)}, f32[4,16,64,64]{3,2,1,0:T(8,128)S(1)}, f32[4,16]{1,0:T(4,128)S(1)}, ...), condition=%wide.region_3.4_spmd.clone, body=%wide.region_2.3_spmd.clone.sunk | while | flops 196611 | bytes 1835743 | solution.py:74
  103.0 1.2 bitcast_dynamic-update-slice_fusion.4
  104.2 1.2 bitcast_dynamic-update-slice_fusion.4
  105.4 1.2 bitcast_dynamic-update-slice_fusion.4
  106.7 1.2 bitcast_dynamic-update-slice_fusion.4
  109.4 2.9 copy.30
  112.3 17.2 %all-gather.2 = f32[16,1,16]{2,1,0:T(1,128)S(1)} all-gather(f32[1,1,16]{2,1,0:T(1,128)S(1)} %slice_bitcast_fusion.3), channel_id=1, replica_groups=mesh['date'=16,'space'=8] {'date'}, dimensions={0}, use_global_device_ids=true | all-gather | bytes 1088 | tf_op jit(solution)/shard_map/all_gather | solution.py:13
  129.6 51.7 %all-gather.7.cloned.1.call-done = f32[256,64,64]{2,1,0:T(8,128)} async-done(((f32[16,64,64]{2,1,0:T(8,128)}), f32[256,64,64]{2,1,0:T(8,128)}) %all-gather.7.cloned.1.call-update) | async-done | bytes 4194320 | tf_op jit(solution)/shard_map/all_gather | solution.py:13
  181.2 18.2 %while.55 = (s32[]{:T(128)}, f32[16,64,64]{2,1,0:T(8,128)S(1)}, s32[]{:T(128)}, f32[16,16]{1,0:T(8,128)S(1)}, f32[16,16,64,64]{3,2,1,0:T(8,128)}, /*index=5*/s32[]{:T(128)}, s32[]{:T(128)}) while((s32[]{:T(128)}, f32[16,64,64]{2,1,0:T(8,128)S(1)}, s32[]{:T(128)}, f32[16,16]{1,0:T(8,128)S(1)}, f32[16,16,64,64]{3,2,1,0:T(8,128)}, ...), condition=%wide.region_6.7_spmd.clone, body=%wide.region_5.6_spmd.clone.sunk | while | flops 262148 | bytes 786729 | solution.py:22
  182.4 1.2 fusion.76
  183.6 1.2 fusion.76
  184.9 1.2 fusion.76
  186.1 1.2 fusion.76
  187.3 1.2 fusion.76
  188.5 1.2 fusion.76
  189.7 1.2 fusion.76
  190.9 1.2 fusion.76
  192.1 1.2 fusion.76
  193.4 1.2 fusion.76
  194.6 1.2 fusion.76
  195.8 1.2 fusion.76
  197.0 1.2 fusion.76
  198.2 1.2 fusion.76
  199.4 2.7 fusion.35
  202.7 1.3 copy-done.5
  204.1 2.7 fusion.14
  206.8 6.8 %fusion.4 = f32[4,256,3072]{2,1,0:T(8,128)S(1)} fusion(bf16[2,1024,3072]{2,1,0:T(8,128)(2,1)S(1)} %bitcast.127, bf16[4,256,1024]{2,1,0:T(8,128)(2,1)S(1)} %get-tuple-element.384, f32[1024]{0:T(1024)S(1)} %bitcast.124, f32[4,256]{1,0:T(4,128)S(1)} %add_rsqrt_fusion.2), kind=kOutput, calls=%fused_computation.24 | convolution fusion | flops 6446645248 | bytes 20979712 | tf_op jit(solution)/shard_map/dot_general | solution.py:42
  213.6 5.1 %fusion.28 = (bf16[4,256,1024]{2,1,0:T(8,128)(2,1)}, bf16[4,256,1024]{2,1,0:T(8,128)(2,1)}) fusion(f32[4,256,3072]{2,1,0:T(8,128)S(1)} %fusion.4, f32[4,256]{1,0:T(4,128)S(1)} %convert_element_type.59), kind=kLoop, calls=%fused_computation.54 | loop fusion | flops 11534336 | bytes 12587008 | tf_op jit(solution)/shard_map/convert_element_type | solution.py:55
  218.7 1.6 slice.112
  220.4 2.8 copy.33
  223.2 3.9 copy.34
  227.2 3.6 fusion.62
  231.1 63.4 %all-reduce.5.cloned.1.call-done = f32[4,16,64,64]{3,2,1,0:T(8,128)} async-done(((f32[4,16,64,64]{3,2,1,0:T(8,128)}), f32[4,16,64,64]{3,2,1,0:T(8,128)}) %all-reduce.5.cloned.1.call-update) | async-done | bytes 1048592 | tf_op jit(solution)/shard_map/psum | solution.py:66
  294.7 4.9 %while.56 = (s32[]{:T(128)}, f32[16,64,64]{2,1,0:T(8,128)S(1)}, f32[4,16,64,64]{3,2,1,0:T(8,128)S(1)}, f32[4,16]{1,0:T(4,128)S(1)}, f32[4,16,64,64]{3,2,1,0:T(8,128)}, /*index=5*/s32[]{:T(128)}, s32[]{:T(128)}) while((s32[]{:T(128)}, f32[16,64,64]{2,1,0:T(8,128)S(1)}, f32[4,16,64,64]{3,2,1,0:T(8,128)S(1)}, ...), condition=%wide.region_11.12_spmd.clone, body=%wide.region_10.11_spmd.clone.sunk | while | flops 196611 | bytes 1835743 | solution.py:74
  294.7 1.2 bitcast_dynamic-update-slice_fusion.5
  296.0 1.2 bitcast_dynamic-update-slice_fusion.5
  297.2 1.2 bitcast_dynamic-update-slice_fusion.5
  298.4 1.2 bitcast_dynamic-update-slice_fusion.5
  300.6 16.6 %all-gather.3 = f32[16,1,16]{2,1,0:T(1,128)S(1)} all-gather(f32[1,1,16]{2,1,0:T(1,128)S(1)} %slice_bitcast_fusion.2), channel_id=1, replica_groups=mesh['date'=16,'space'=8] {'date'}, dimensions={0}, use_global_device_ids=true | all-gather | bytes 1088 | tf_op jit(solution)/shard_map/all_gather | solution.py:13
  317.2 2.9 copy.35
  320.1 52.9 %all-gather.9.cloned.1.call-done = f32[256,64,64]{2,1,0:T(8,128)} async-done(((f32[16,64,64]{2,1,0:T(8,128)}), f32[256,64,64]{2,1,0:T(8,128)}) %all-gather.9.cloned.1.call-update) | async-done | bytes 4194320 | tf_op jit(solution)/shard_map/all_gather | solution.py:13
  373.0 18.2 %while.57 = (s32[]{:T(128)}, f32[16,64,64]{2,1,0:T(8,128)S(1)}, s32[]{:T(128)}, f32[16,16]{1,0:T(8,128)S(1)}, f32[16,16,64,64]{3,2,1,0:T(8,128)}, /*index=5*/s32[]{:T(128)}, s32[]{:T(128)}) while((s32[]{:T(128)}, f32[16,64,64]{2,1,0:T(8,128)S(1)}, s32[]{:T(128)}, f32[16,16]{1,0:T(8,128)S(1)}, f32[16,16,64,64]{3,2,1,0:T(8,128)}, ...), condition=%wide.region_14.15_spmd.clone, body=%wide.region_13.14_spmd.clone.sunk | while | flops 262148 | bytes 786729 | solution.py:22
  374.2 1.2 fusion.78
  375.4 1.2 fusion.78
  376.6 1.2 fusion.78
  377.8 1.2 fusion.78
  379.0 1.2 fusion.78
  380.2 1.2 fusion.78
  381.5 1.2 fusion.78
  383.9 1.2 fusion.78
  385.1 1.2 fusion.78
  386.3 1.2 fusion.78
  390.0 1.2 fusion.78
  391.1 2.6 fusion.32
  394.3 1.6 copy-done.10
  396.6 3.7 fusion.17
  (104 shorter events, 12.8 us)
Async XLA Ops:
  6.5 3.0 copy-start.4
  6.5 3.0 copy-start.7
  6.5 96.2 %all-reduce.3.cloned.1.call-start = ((), (), s32[]{:S(2)}) async-start(), calls=%async_computation | async-start | bytes 4194304 | tf_op jit(solution)/shard_map/psum | solution.py:66
  35.6 0.7 copy-start.8
  35.6 145.6 %all-gather.7.cloned.1.call-start = ((), (), s32[]{:S(2)}) async-start(), calls=%async_computation.2 | async-start | bytes 8912896 | tf_op jit(solution)/shard_map/all_gather | solution.py:13
  107.9 0.8 copy-start
  107.9 1.5 copy-start.3
  108.7 185.8 %all-reduce.5.cloned.1.call-start = ((), (), s32[]{:S(2)}) async-start(), calls=%async_computation.1 | async-start | bytes 4194304 | tf_op jit(solution)/shard_map/psum | solution.py:66
  109.4 2.9 copy-start.6
  199.4 3.3 copy-start.9
  199.4 7.4 %slice-start = ((s8[12582912]{0:T(1024)(128)(4,1)}), s8[4194304]{0:T(1024)(128)(4,1)S(1)}, s32[]{:S(2)}) async-start(s8[12582912]{0:T(1024)(128)(4,1)} %bitcast.126), calls=%async_computation.4 | async-start | bytes 8388608
  202.2 1.9 copy-start.5
  202.2 4.6 %slice-start.1 = ((s8[12582912]{0:T(1024)(128)(4,1)}), s8[4194304]{0:T(1024)(128)(4,1)S(1)}, s32[]{:S(2)}) async-start(s8[12582912]{0:T(1024)(128)(4,1)} %bitcast.126), calls=%async_computation.5 | async-start | bytes 8388608
  204.1 2.8 slice-start.2
  206.8 6.8 %copy-start.11 = (bf16[4,256,1024]{2,1,0:T(8,128)(2,1)}, bf16[4,256,1024]{2,1,0:T(8,128)(2,1)S(1)}, u32[]{:S(2)}) copy-start(bf16[4,256,1024]{2,1,0:T(8,128)(2,1)S(1)} %get-tuple-element.384) | copy-start | bytes 6291460
  230.8 142.2 %all-gather.9.cloned.1.call-start = ((), (), s32[]{:S(2)}) async-start(), calls=%async_computation.3 | async-start | bytes 8912896 | tf_op jit(solution)/shard_map/all_gather | solution.py:13
  299.6 0.8 copy-start.1
  299.6 17.6 %copy-start.2 = (f32[4,16,64,64]{3,2,1,0:T(8,128)}, f32[4,16,64,64]{3,2,1,0:T(8,128)S(1)}, u32[]{:S(2)}) copy-start(f32[4,16,64,64]{3,2,1,0:T(8,128)S(1)} %get-tuple-element.252) | copy-start | bytes 3145732
  393.7 2.2 copy-start.10
  393.8 2.9 copy-start.12
Sparse Core Ops, SparseCore 0:
  35.7 66.9 all-reduce.2
  108.8 72.3 all-gather.6
  230.9 63.4 all-reduce.4
  300.6 72.3 all-gather.8
where the time goes:
time: 409 us; the launch traced here: 407 us
  waiting for transfers between devices  234 us (57%)
  other arithmetic  58.1 us (14%)
  matrix products  34.5 us (8%)
  blocking collectives  33.8 us (8%)
  local copies, waits for them, and re-layouts  30.9 us (8%)
  between operations  13.5 us (3%)
    psum x2, waiting for transfers between devices, shards(): kv = lax.psum(pairing_partial, 'space')  130 us
    all_gather x2, waiting for transfers between devices, carried_in(): pieces = jax.tree.map(lambda part: lax.all_gather(part, axis), value)  105 us
    select_n x30, other arithmetic, step(): jnp.where(position < mine, new, old)  35.2 us
    all_gather x2, blocking collectives, carried_in(): pieces = jax.tree.map(lambda part: lax.all_gather(part, axis), value)  33.8 us
    dot_general x2, matrix products, shards(): jnp.dot(normalized_output.reshape(-1, width), qkv_weight[layer], preferre...  15.6 us
    slice x4, local copies, waits for them, and re-layouts, shards(): proj[:, :, 2 * width:].astype(jnp.bfloat16)  11.2 us
    convert_element_type x2, other arithmetic, shards(): key = (feature(proj[:, :, width:2 * width]) * flag_f).astype(jnp.bfloat16...  10.2 us
    dynamic_update_slice x8, other arithmetic, shards(): last_state, local_states = lax.scan(advance, start, (kv, persist_factor))  9.48 us
  transfers between devices with their start and end apart: 4, of which 4 were waited for; matrix products, arithmetic and copies ran while one was open for 1% of the time, Pallas kernels for 0%

commit v1 on v0

--- a/solution.py
+++ b/solution.py
@@ -63,7 +63,13 @@
         pairing_partial = jnp.einsum(
             "tshe,tshf->thef", key, value, preferred_element_type=jnp.float32
         )
-        kv = lax.psum(pairing_partial, "space")
+        size_here = lax.axis_size("space")
+        kv = pairing_partial
+        for jj in [
+            [(p, p ^ idx) for p in range(size_here)] for idx in (1, 2, 4, 8, 16) if idx < size_here
+        ]:
+            current_block = lax.ppermute(kv, "space", jj)
+            kv = kv + current_block
         persist_factor = decay[layer]
 
         def advance(state, inputs):

time: 409 us -> 485 us (1.19)
  waiting for transfers between devices: 234 us -> 294 us
  starting transfers between devices: 0.35 us -> 11.4 us
  other arithmetic: 58.1 us -> 63.3 us
    ppermute x0 -> x6, waiting for transfers between devices: none -> 188 us  [shards(): current_block = lax.ppermute(kv, 'space', jj)]
    psum x2 -> x0, waiting for transfers between devices: 130 us -> none  [shards(): kv = lax.psum(pairing_partial, 'space')]
    ppermute x0 -> x6, starting transfers between devices: none -> 11.3 us  [shards(): current_block = lax.ppermute(kv, 'space', jj)]
    add x0 -> x6, other arithmetic: none -> 7.11 us  [shards(): kv = kv + current_block]
  transfers between devices with their start and end apart: 4 -> 8, of which waited for: 4 -> 8; matrix products, arithmetic and copies ran while one was open for 1% -> 1% of each run, Pallas kernels for 0% -> 0%
where the time goes in v1:
time: 485 us; the launch traced here: 483 us
  waiting for transfers between devices  294 us (61%)
  other arithmetic  63.3 us (13%)
  blocking collectives  34.6 us (7%)
  local copies, waits for them, and re-layouts  32.5 us (7%)
  matrix products  31.9 us (7%)
  between operations  13.8 us (3%)
  starting transfers between devices  11.4 us (2%)
    ppermute x6, waiting for transfers between devices, shards(): current_block = lax.ppermute(kv, 'space', jj)  188 us
    all_gather x2, waiting for transfers between devices, carried_in(): pieces = jax.tree.map(lambda part: lax.all_gather(part, axis), value)  106 us
    select_n x30, other arithmetic, step(): jnp.where(position < mine, new, old)  35.2 us
    all_gather x2, blocking collectives, carried_in(): pieces = jax.tree.map(lambda part: lax.all_gather(part, axis), value)  34.6 us
    dot_general x2, matrix products, shards(): jnp.dot(normalized_output.reshape(-1, width), qkv_weight[layer], preferre...  15.6 us
    ppermute x6, starting transfers between devices, shards(): current_block = lax.ppermute(kv, 'space', jj)  11.3 us
    slice x4, local copies, waits for them, and re-layouts, shards(): proj[:, :, 2 * width:].astype(jnp.bfloat16)  11.2 us
    convert_element_type x2, other arithmetic, shards(): key = (feature(proj[:, :, width:2 * width]) * flag_f).astype(jnp.bfloat16...  10.3 us
  transfers between devices with their start and end apart: 8, of which 8 were waited for; matrix products, arithmetic and copies ran while one was open for 1% of the time, Pallas kernels for 0%

profile of v1, /device:TPU:1, one launch (start us, length us, event | category | flops | bytes accessed | tf_op | source)
XLA Modules:
  0.0 482.5 jit_solution(2082037682731890510)
XLA Ops:
  7.4 2.1 fusion.10
  9.5 8.9 %fusion.6 = f32[4,256,3072]{2,1,0:T(8,128)S(1)} fusion(bf16[2,1024,3072]{2,1,0:T(8,128)(2,1)} %param.17, bf16[4,256,1024]{2,1,0:T(8,128)(2,1)S(1)} %copy-done.4, f32[1024]{0:T(1024)S(1)} %bitcast.125, f32[4,256]{1,0:T(4,128)S(1)} %add_rsqrt_fusion.3), kind=kOutput, calls=%fused_computation.26 | convolution fusion | flops 6446645248 | bytes 20979712 | tf_op jit(solution)/shard_map/dot_general | solution.py:42
  18.4 1.7 slice.113
  20.1 5.1 %fusion.21 = (bf16[4,256,1024]{2,1,0:T(8,128)(2,1)}, bf16[4,256,1024]{2,1,0:T(8,128)(2,1)}) fusion(f32[4,256,3072]{2,1,0:T(8,128)S(1)} %fusion.6, f32[4,256]{1,0:T(4,128)S(1)} %convert_element_type.59), kind=kLoop, calls=%fused_computation.47 | loop fusion | flops 11534336 | bytes 12587008 | tf_op jit(solution)/shard_map/convert_element_type | solution.py:55
  25.2 2.8 copy.28
  28.1 3.9 copy.29
  32.0 2.3 fusion.61
  34.3 1.5 collective-permute-start
  35.8 3.8 collective-permute-done
  40.1 1.5 collective-permute-start.1
  41.6 45.4 %collective-permute-done.1 = f32[4,16,64,64]{3,2,1,0:T(8,128)S(1)} collective-permute-done((f32[4,16,64,64]{3,2,1,0:T(8,128)S(1)}, f32[4,16,64,64]{3,2,1,0:T(8,128)S(1)}, u32[]{:S(2)}, u32[]{:S(2)}) %collective-permute-start.1) | collective-permute-done | bytes 1048608 | tf_op jit(solution)/shard_map/ppermute | solution.py:71
  87.4 3.1 collective-permute-start.2
  90.5 44.7 %collective-permute-done.2 = f32[4,16,64,64]{3,2,1,0:T(8,128)} collective-permute-done((f32[4,16,64,64]{3,2,1,0:T(8,128)S(1)}, f32[4,16,64,64]{3,2,1,0:T(8,128)}, u32[]{:S(2)}, u32[]{:S(2)}) %collective-permute-start.2) | collective-permute-done | bytes 1048608 | tf_op jit(solution)/shard_map/ppermute | solution.py:71
  135.2 2.6 add.148
  137.8 1.6 broadcast.94.clone
  139.4 3.8 while.54
  144.1 2.9 copy.30
  147.1 18.5 %all-gather.2 = f32[16,1,16]{2,1,0:T(1,128)S(1)} all-gather(f32[1,1,16]{2,1,0:T(1,128)S(1)} %slice_bitcast_fusion.3), channel_id=1, replica_groups=mesh['date'=16,'space'=8] {'date'}, dimensions={0}, use_global_device_ids=true | all-gather | bytes 1088 | tf_op jit(solution)/shard_map/all_gather | solution.py:13
  165.6 53.2 %all-gather.7.cloned.1.call-done = f32[256,64,64]{2,1,0:T(8,128)} async-done(((f32[16,64,64]{2,1,0:T(8,128)}), f32[256,64,64]{2,1,0:T(8,128)}) %all-gather.7.cloned.1.call-update) | async-done | bytes 4194320 | tf_op jit(solution)/shard_map/all_gather | solution.py:13
  218.8 18.2 %while.55 = (s32[]{:T(128)}, f32[16,64,64]{2,1,0:T(8,128)S(1)}, s32[]{:T(128)}, f32[16,16]{1,0:T(8,128)S(1)}, f32[16,16,64,64]{3,2,1,0:T(8,128)}, /*index=5*/s32[]{:T(128)}, s32[]{:T(128)}) while((s32[]{:T(128)}, f32[16,64,64]{2,1,0:T(8,128)S(1)}, s32[]{:T(128)}, f32[16,16]{1,0:T(8,128)S(1)}, f32[16,16,64,64]{3,2,1,0:T(8,128)}, ...), condition=%wide.region_5.6_spmd.clone, body=%wide.region_4.5_spmd.clone.sunk | while | flops 262148 | bytes 786729 | solution.py:22
  220.0 1.2 fusion.76
  221.2 1.2 fusion.76
  222.4 1.2 fusion.76
  223.6 1.2 fusion.76
  224.8 1.2 fusion.76
  226.1 1.2 fusion.76
  227.3 1.2 fusion.76
  228.5 1.2 fusion.76
  229.7 1.2 fusion.76
  230.9 1.2 fusion.76
  232.1 1.2 fusion.76
  235.8 1.2 fusion.76
  237.0 2.7 fusion.35
  240.3 1.3 copy-done.5
  241.6 2.7 fusion.14
  244.4 6.8 %fusion.4 = f32[4,256,3072]{2,1,0:T(8,128)S(1)} fusion(bf16[2,1024,3072]{2,1,0:T(8,128)(2,1)S(1)} %bitcast.127, bf16[4,256,1024]{2,1,0:T(8,128)(2,1)S(1)} %get-tuple-element.384, f32[1024]{0:T(1024)S(1)} %bitcast.124, f32[4,256]{1,0:T(4,128)S(1)} %add_rsqrt_fusion.2), kind=kOutput, calls=%fused_computation.24 | convolution fusion | flops 6446645248 | bytes 20979712 | tf_op jit(solution)/shard_map/dot_general | solution.py:42
  251.2 5.1 %fusion.28 = (bf16[4,256,1024]{2,1,0:T(8,128)(2,1)}, bf16[4,256,1024]{2,1,0:T(8,128)(2,1)}) fusion(f32[4,256,3072]{2,1,0:T(8,128)S(1)} %fusion.4, f32[4,256]{1,0:T(4,128)S(1)} %convert_element_type.59), kind=kLoop, calls=%fused_computation.54 | loop fusion | flops 11534336 | bytes 12587008 | tf_op jit(solution)/shard_map/convert_element_type | solution.py:55
  256.3 1.6 slice.112
  257.9 2.8 copy.33
  260.8 3.9 copy.34
  264.7 2.3 fusion.62
  268.1 3.8 collective-permute-done.3
  272.5 1.3 collective-permute-start.4
  273.8 45.6 %collective-permute-done.4 = f32[4,16,64,64]{3,2,1,0:T(8,128)S(1)} collective-permute-done((f32[4,16,64,64]{3,2,1,0:T(8,128)S(1)}, f32[4,16,64,64]{3,2,1,0:T(8,128)S(1)}, u32[]{:S(2)}, u32[]{:S(2)}) %collective-permute-start.4) | collective-permute-done | bytes 1048608 | tf_op jit(solution)/shard_map/ppermute | solution.py:71
  319.8 2.8 collective-permute-start.5
  322.6 44.8 %collective-permute-done.5 = f32[4,16,64,64]{3,2,1,0:T(8,128)} collective-permute-done((f32[4,16,64,64]{3,2,1,0:T(8,128)S(1)}, f32[4,16,64,64]{3,2,1,0:T(8,128)}, u32[]{:S(2)}, u32[]{:S(2)}) %collective-permute-start.5) | collective-permute-done | bytes 1048608 | tf_op jit(solution)/shard_map/ppermute | solution.py:71
  367.4 2.6 add.157
  370.1 1.6 broadcast.94
  371.6 3.8 while.56
  376.4 16.1 %all-gather.3 = f32[16,1,16]{2,1,0:T(1,128)S(1)} all-gather(f32[1,1,16]{2,1,0:T(1,128)S(1)} %slice_bitcast_fusion.2), channel_id=1, replica_groups=mesh['date'=16,'space'=8] {'date'}, dimensions={0}, use_global_device_ids=true | all-gather | bytes 1088 | tf_op jit(solution)/shard_map/all_gather | solution.py:13
  392.5 2.9 copy.35
  395.3 53.0 %all-gather.9.cloned.1.call-done = f32[256,64,64]{2,1,0:T(8,128)} async-done(((f32[16,64,64]{2,1,0:T(8,128)}), f32[256,64,64]{2,1,0:T(8,128)}) %all-gather.9.cloned.1.call-update) | async-done | bytes 4194320 | tf_op jit(solution)/shard_map/all_gather | solution.py:13
  448.3 18.2 %while.57 = (s32[]{:T(128)}, f32[16,64,64]{2,1,0:T(8,128)S(1)}, s32[]{:T(128)}, f32[16,16]{1,0:T(8,128)S(1)}, f32[16,16,64,64]{3,2,1,0:T(8,128)}, /*index=5*/s32[]{:T(128)}, s32[]{:T(128)}) while((s32[]{:T(128)}, f32[16,64,64]{2,1,0:T(8,128)S(1)}, s32[]{:T(128)}, f32[16,16]{1,0:T(8,128)S(1)}, f32[16,16,64,64]{3,2,1,0:T(8,128)}, ...), condition=%wide.region_12.13_spmd.clone, body=%wide.region_11.12_spmd.clone.sunk | while | flops 262148 | bytes 786729 | solution.py:22
  452.0 1.2 fusion.78
  453.2 1.2 fusion.78
  454.4 1.2 fusion.78
  458.0 1.2 fusion.78
  459.2 1.2 fusion.78
  460.5 1.2 fusion.78
  464.1 1.2 fusion.78
  465.3 1.2 fusion.78
  466.5 2.6 fusion.32
  469.6 1.6 copy-done.10
  472.0 3.7 fusion.17
  (116 shorter events, 27.2 us)
Async XLA Ops:
  6.5 3.0 copy-start.4
  6.5 3.0 copy-start.7
  6.5 212.2 %all-gather.7.cloned.1.call-start = ((), (), s32[]{:S(2)}) async-start(), calls=%async_computation | async-start | bytes 8912896 | tf_op jit(solution)/shard_map/all_gather | solution.py:13
  34.3 5.2 %collective-permute-start = (f32[4,16,64,64]{3,2,1,0:T(8,128)S(1)}, f32[4,16,64,64]{3,2,1,0:T(8,128)S(1)}, u32[]{:S(2)}, u32[]{:S(2)}) collective-permute-start(f32[4,16,64,64]{3,2,1,0:T(8,128)S(1)} %fusion.61), channel_id=1, source_target_pairs={{0,1},{1,0},{2,3},{3,2},{4,5},{5,4},{6,7},{7,6},{8,9},{9,8},{10,11... | collective-permute-start | bytes 3145736 | tf_op jit(solution)/shard_map/ppermute | solution.py:71
  40.1 50.4 %copy-start.8 = (f32[2,4,16]{2,1,0:T(4,128)S(1)}, f32[2,4,16]{2,1,0:T(4,128)}, u32[]{:S(2)}) copy-start(f32[2,4,16]{2,1,0:T(4,128)} %param.21) | copy-start | bytes 1540
  40.1 46.9 %collective-permute-start.1 = (f32[4,16,64,64]{3,2,1,0:T(8,128)S(1)}, f32[4,16,64,64]{3,2,1,0:T(8,128)S(1)}, u32[]{:S(2)}, u32[]{:S(2)}) collective-permute-start(f32[4,16,64,64]{3,2,1,0:T(8,128)S(1)} %add.146), channel_id=1, source_target_pairs={{0,2},{1,3},{2,0},{3,1},{4,6},{5,7},{6,4},{7,5},{8,10},{9,11},{10,... | collective-permute-start | bytes 3145736 | tf_op jit(solution)/shard_map/ppermute | solution.py:71
  87.4 3.1 copy-start.2
  87.4 47.8 %collective-permute-start.2 = (f32[4,16,64,64]{3,2,1,0:T(8,128)S(1)}, f32[4,16,64,64]{3,2,1,0:T(8,128)}, u32[]{:S(2)}, u32[]{:S(2)}) collective-permute-start(f32[4,16,64,64]{3,2,1,0:T(8,128)S(1)} %add.147), channel_id=1, source_target_pairs={{0,4},{1,5},{2,6},{3,7},{4,0},{5,1},{6,2},{7,3},{8,12},{9,13},{10,... | collective-permute-start | bytes 3145736 | tf_op jit(solution)/shard_map/ppermute | solution.py:71
  143.1 0.8 copy-start
  144.0 304.3 %all-gather.9.cloned.1.call-start = ((), (), s32[]{:S(2)}) async-start(), calls=%async_computation.1 | async-start | bytes 8912896 | tf_op jit(solution)/shard_map/all_gather | solution.py:13
  144.1 2.9 copy-start.6
  237.0 3.3 copy-start.9
  237.0 7.4 %slice-start = ((s8[12582912]{0:T(1024)(128)(4,1)}), s8[4194304]{0:T(1024)(128)(4,1)S(1)}, s32[]{:S(2)}) async-start(s8[12582912]{0:T(1024)(128)(4,1)} %bitcast.126), calls=%async_computation.2 | async-start | bytes 8388608
  239.7 1.9 copy-start.5
  239.8 4.6 slice-start.1
  241.6 2.8 slice-start.2
  244.3 6.8 %copy-start.11 = (bf16[4,256,1024]{2,1,0:T(8,128)(2,1)}, bf16[4,256,1024]{2,1,0:T(8,128)(2,1)S(1)}, u32[]{:S(2)}) copy-start(bf16[4,256,1024]{2,1,0:T(8,128)(2,1)S(1)} %get-tuple-element.384) | copy-start | bytes 6291460
  267.0 4.9 %collective-permute-start.3 = (f32[4,16,64,64]{3,2,1,0:T(8,128)S(1)}, f32[4,16,64,64]{3,2,1,0:T(8,128)S(1)}, u32[]{:S(2)}, u32[]{:S(2)}) collective-permute-start(f32[4,16,64,64]{3,2,1,0:T(8,128)S(1)} %fusion.62), channel_id=1, source_target_pairs={{0,1},{1,0},{2,3},{3,2},{4,5},{5,4},{6,7},{7,6},{8,9},{9,8},{10,11... | collective-permute-start | bytes 3145736 | tf_op jit(solution)/shard_map/ppermute | solution.py:71
  272.5 46.9 %collective-permute-start.4 = (f32[4,16,64,64]{3,2,1,0:T(8,128)S(1)}, f32[4,16,64,64]{3,2,1,0:T(8,128)S(1)}, u32[]{:S(2)}, u32[]{:S(2)}) collective-permute-start(f32[4,16,64,64]{3,2,1,0:T(8,128)S(1)} %add.155), channel_id=1, source_target_pairs={{0,2},{1,3},{2,0},{3,1},{4,6},{5,7},{6,4},{7,5},{8,10},{9,11},{10,... | collective-permute-start | bytes 3145736 | tf_op jit(solution)/shard_map/ppermute | solution.py:71
  319.8 2.8 copy-start.3
  319.8 47.6 %collective-permute-start.5 = (f32[4,16,64,64]{3,2,1,0:T(8,128)S(1)}, f32[4,16,64,64]{3,2,1,0:T(8,128)}, u32[]{:S(2)}, u32[]{:S(2)}) collective-permute-start(f32[4,16,64,64]{3,2,1,0:T(8,128)S(1)} %add.156), channel_id=1, source_target_pairs={{0,4},{1,5},{2,6},{3,7},{4,0},{5,1},{6,2},{7,3},{8,12},{9,13},{10,... | collective-permute-start | bytes 3145736 | tf_op jit(solution)/shard_map/ppermute | solution.py:71
  375.4 0.8 copy-start.1
  469.1 2.2 copy-start.10
  469.1 2.9 copy-start.12
Sparse Core Ops, SparseCore 0:
  144.1 74.6 all-gather.6
  376.4 71.8 all-gather.8
